TPU v7x, 32 devices: a whole 2x2x4 slice. The times are simulated.
32 devices in a mesh: dp: 4 (over y, core), row: 2 (over x), col: 4 (over z).
Axes of the slice: x: 2, y: 2, z: 4, core: 2. Of those that a mesh axis runs over, the one named last changes fastest.
Arguments:
- block_in: bfloat16 [8192, 1536], P(('dp', 'row', 'col')), may hold values from -6 to 6
- out_grad: bfloat16 [8192, 1536], P(('dp', 'row', 'col')), may hold values from -6 to 6
- norm_gain: float32 [1536], replicated, may hold values from 0.5 to 1.5
- first_norm_gain: float32 [1536], replicated, may hold values from -28 to 28
- second_norm_gain: float32 [1536], replicated, may hold values from 16.384 to 163.84
- input_proj: float32 [1536, 6144], P('dp', ('row', 'col')), may hold values from -0.18371173 to 0.18371173
- first_input_proj: float32 [1536, 6144], P('dp', ('row', 'col')), may hold values from -28 to 28
- second_input_proj: float32 [1536, 6144], P('dp', ('row', 'col')), may hold values from 16.384 to 163.84
- state_proj: float32 [1536, 256], P(('dp', 'row', 'col')), may hold values from -0.15625 to 0.15625
- first_state_proj: float32 [1536, 256], P(('dp', 'row', 'col')), may hold values from -28 to 28
- second_state_proj: float32 [1536, 256], P(('dp', 'row', 'col')), may hold values from 16.384 to 163.84
- step_proj: float32 [1536, 48], P(('dp', 'row', 'col')), may hold values from -0.15625 to 0.15625
- first_step_proj: float32 [1536, 48], P(('dp', 'row', 'col')), may hold values from -28 to 28
- second_step_proj: float32 [1536, 48], P(('dp', 'row', 'col')), may hold values from 16.384 to 163.84
- conv_taps: float32 [5, 3328], replicated, may hold values from -0.5 to 0.5
- first_conv_taps: float32 [5, 3328], replicated, may hold values from -28 to 28
- second_conv_taps: float32 [5, 3328], replicated, may hold values from 16.384 to 163.84
- head_coef: float32 [3, 48], replicated, may hold values from -7 to 3
- first_head_coef: float32 [3, 48], replicated, may hold values from -28 to 28
- second_head_coef: float32 [3, 48], replicated, may hold values from 16.384 to 163.84
- gated_gain: float32 [3072], replicated, may hold values from 0.5 to 1.5
- first_gated_gain: float32 [3072], replicated, may hold values from -28 to 28
- second_gated_gain: float32 [3072], replicated, may hold values from 16.384 to 163.84
- output_proj: float32 [3072, 1536], P(('row', 'col'), 'dp'), may hold values from -0.109375 to 0.109375
- first_output_proj: float32 [3072, 1536], P(('row', 'col'), 'dp'), may hold values from -28 to 28
- second_output_proj: float32 [3072, 1536], P(('row', 'col'), 'dp'), may hold values from 16.384 to 163.84
Outputs:
- block_out: bfloat16 [8192, 1536], P(('dp', 'row', 'col'))
- input_grad: float32 [8192, 1536], P(('dp', 'row', 'col'))
- grad_norm_gain: float32 [1536], replicated
- grad_input_proj: float32 [1536, 6144], P('dp', ('row', 'col'))
- grad_state_proj: float32 [1536, 256], P(('dp', 'row', 'col'))
- grad_step_proj: float32 [1536, 48], P(('dp', 'row', 'col'))
- grad_conv_taps: float32 [5, 3328], replicated
- grad_head_coef: float32 [3, 48], replicated
- grad_gated_gain: float32 [3072], replicated
- grad_output_proj: float32 [3072, 1536], P(('row', 'col'), 'dp')
- new_norm_gain: float32 [1536], replicated
- new_first_norm_gain: float32 [1536], replicated
- new_second_norm_gain: float32 [1536], replicated
- new_input_proj: float32 [1536, 6144], P('dp', ('row', 'col'))
- new_first_input_proj: float32 [1536, 6144], P('dp', ('row', 'col'))
- new_second_input_proj: float32 [1536, 6144], P('dp', ('row', 'col'))
- new_state_proj: float32 [1536, 256], P(('dp', 'row', 'col'))
- new_first_state_proj: float32 [1536, 256], P(('dp', 'row', 'col'))
- new_second_state_proj: float32 [1536, 256], P(('dp', 'row', 'col'))
- new_step_proj: float32 [1536, 48], P(('dp', 'row', 'col'))
- new_first_step_proj: float32 [1536, 48], P(('dp', 'row', 'col'))
- new_second_step_proj: float32 [1536, 48], P(('dp', 'row', 'col'))
- new_conv_taps: float32 [5, 3328], replicated
- new_first_conv_taps: float32 [5, 3328], replicated
- new_second_conv_taps: float32 [5, 3328], replicated
- new_head_coef: float32 [3, 48], replicated
- new_first_head_coef: float32 [3, 48], replicated
- new_second_head_coef: float32 [3, 48], replicated
- new_gated_gain: float32 [3072], replicated
- new_first_gated_gain: float32 [3072], replicated
- new_second_gated_gain: float32 [3072], replicated
- new_output_proj: float32 [3072, 1536], P(('row', 'col'), 'dp')
- new_first_output_proj: float32 [3072, 1536], P(('row', 'col'), 'dp')
- new_second_output_proj: float32 [3072, 1536], P(('row', 'col'), 'dp')
All inputs are finite; a program needn't handle non-finite values.
Results may differ from a plain program's by a relative error of at most 0.0034.
The roundings to bfloat16 on the way count: a program that leaves them out, or rounds other values in their place, can miss the bound.
Values may be sent and summed in bfloat16 or wider, within the bound.
No kernel may reach another device: no remote copies, remote signals or barrier semaphores. Data moves between devices by JAX's collectives and lax.ppermute only.
A program may use at most 192 MiB of HBM per device.

v0:
```python
import jax
import jax.numpy as jnp
from jax import lax
from jax.sharding import PartitionSpec as P

SPAN = 256
SEQ_LEN = 1024
ADAM_STEP = 4
PRECISE = lax.Precision.HIGHEST
NORM_EPS = 1e-05
BETA_ONE = 0.9
BETA_TWO = 0.95
ADAM_EPS = 1e-08
MATRIX_RATE = 0.003
VECTOR_RATE = 0.1
WEIGHT_DECAY = 0.1


def causal_conv(values, filters):
    length = values.shape[0]
    padded = jnp.pad(values, ((3, 0), (0, 0)))
    summed = filters[4][None, :] + jnp.zeros_like(values)
    for offset in range(4):
        summed = summed + filters[offset][None, :] * padded[offset : offset + length]
    return summed


def span_scan(values, deltas, rates, key_rows, query_rows):
    length, head_count, head_width = values.shape
    states = key_rows.shape[1]
    blocks = length // SPAN
    values = values.reshape(blocks, SPAN, head_count, head_width)
    deltas = deltas.reshape(blocks, SPAN, head_count)
    key_rows = key_rows.reshape(blocks, SPAN, states)
    query_rows = query_rows.reshape(blocks, SPAN, states)
    log_decay = jnp.cumsum(deltas * rates[None, None, :], axis=1)
    scores = jnp.einsum("kqn,krn->kqr", query_rows, key_rows, precision=PRECISE)
    causal = jnp.arange(SPAN)[:, None] >= jnp.arange(SPAN)[None, :]
    head_decay = jnp.transpose(log_decay, (0, 2, 1))
    head_deltas = jnp.transpose(deltas, (0, 2, 1))
    spread = head_decay[:, :, :, None] - head_decay[:, :, None, :]
    decays = jnp.exp(jnp.where(causal[None, None, :, :], spread, -jnp.inf))
    mixing = scores[:, None, :, :] * decays * head_deltas[:, :, None, :]
    within = jnp.einsum("khqr,krhp->kqhp", mixing, values, precision=PRECISE)
    to_end = jnp.exp(log_decay[:, -1:, :] - log_decay) * deltas
    produced = jnp.einsum("kqn,kqh,kqhp->khnp", key_rows, to_end, values, precision=PRECISE)
    factors = jnp.exp(log_decay[:, -1, :])
    carried = jnp.zeros((head_count, states, head_width), jnp.float32)
    entering = []
    for number in range(blocks):
        entering.append(carried)
        carried = carried * factors[number][:, None, None] + produced[number]
    entering = jnp.stack(entering)
    across = (
        jnp.einsum("kqn,khnp->kqhp", query_rows, entering, precision=PRECISE)
        * jnp.exp(log_decay)[:, :, :, None]
    )
    return (within + across).reshape(length, head_count, head_width)


def mixer_sequence(gate_part, inputs, state_in, step_raw, conv_inner, conv_state, coefs):
    length = inputs.shape[0]
    head_count = coefs.shape[1]
    head_width = inputs.shape[1] // head_count
    state_size = state_in.shape[1] // 2
    conv_out = jax.nn.silu(causal_conv(inputs, conv_inner))
    state_out = jax.nn.silu(causal_conv(state_in, conv_state))
    deltas = jax.nn.softplus(step_raw + coefs[0][None, :])
    rates = -jnp.exp(coefs[1])
    shaped = conv_out.reshape(length, head_count, head_width)
    result = span_scan(shaped, deltas, rates, state_out[:, :state_size], state_out[:, state_size:])
    result = result + coefs[2][None, :, None] * shaped
    return result.reshape(length, head_count * head_width) * jax.nn.silu(gate_part)


def mixer_all(gate_part, inputs, state_in, step_raw, conv_inner, conv_state, coefs):
    seq_count = inputs.shape[0] // SEQ_LEN

    def sequence(pieces):
        return mixer_sequence(
            pieces[0], pieces[1], pieces[2], pieces[3], conv_inner, conv_state, coefs
        )

    gated = lax.map(
        jax.checkpoint(sequence),
        (
            gate_part.reshape(seq_count, SEQ_LEN, -1),
            inputs.reshape(seq_count, SEQ_LEN, -1),
            state_in.reshape(seq_count, SEQ_LEN, -1),
            step_raw.reshape(seq_count, SEQ_LEN, -1),
        ),
    )
    return gated.reshape(inputs.shape[0], -1)


def adamw(weight, gradient, moment_one, moment_two, step_rate, shrink):
    new_one = BETA_ONE * moment_one + (1.0 - BETA_ONE) * gradient
    new_two = BETA_TWO * moment_two + (1.0 - BETA_TWO) * gradient * gradient
    one_hat = new_one / (1.0 - BETA_ONE**ADAM_STEP)
    two_hat = new_two / (1.0 - BETA_TWO**ADAM_STEP)
    updated = weight - step_rate * (one_hat / (jnp.sqrt(two_hat) + ADAM_EPS) + shrink * weight)
    return (updated, new_one, new_two)


def per_device(
    block_in,
    out_grad,
    norm_gain,
    first_norm_gain,
    second_norm_gain,
    input_proj,
    first_input_proj,
    second_input_proj,
    state_proj,
    first_state_proj,
    second_state_proj,
    step_proj,
    first_step_proj,
    second_step_proj,
    conv_taps,
    first_conv_taps,
    second_conv_taps,
    head_coef,
    first_head_coef,
    second_head_coef,
    gated_gain,
    first_gated_gain,
    second_gated_gain,
    output_proj,
    first_output_proj,
    second_output_proj,
):
    groups = lax.axis_size(("row", "col"))
    place = lax.axis_index(("row", "col"))
    tok_dev = block_in.shape[0]
    group_tok = tok_dev * groups
    inner = gated_gain.shape[0]
    inner_dev = inner // groups
    head_total = head_coef.shape[1]
    heads_dev = head_total // groups
    head_width = inner // head_total
    in_local, out_local = (
        lax.all_gather(input_proj.astype(jnp.bfloat16), "dp", axis=0, tiled=True),
        lax.all_gather(output_proj.astype(jnp.bfloat16), "dp", axis=1, tiled=True),
    )
    state_full, step_full = (
        lax.all_gather(state_proj.astype(jnp.bfloat16), ("dp", "row", "col"), axis=0, tiled=True),
        lax.all_gather(step_proj.astype(jnp.bfloat16), ("dp", "row", "col"), axis=0, tiled=True),
    )
    x_float = block_in.astype(jnp.float32)
    inv_rms = lax.rsqrt(jnp.mean(x_float * x_float, axis=1, keepdims=True) + NORM_EPS)
    normed_in = (x_float * inv_rms * norm_gain[None, :]).astype(jnp.bfloat16)
    state_own = jnp.dot(normed_in, state_full, preferred_element_type=jnp.float32).astype(
        jnp.bfloat16
    )
    step_own = jnp.dot(normed_in, step_full, preferred_element_type=jnp.float32).astype(
        jnp.bfloat16
    )
    normed_all, state_all, step_all, cotangent = (
        lax.all_gather(normed_in, ("row", "col"), axis=0, tiled=True),
        lax.all_gather(state_own, ("row", "col"), axis=0, tiled=True),
        lax.all_gather(step_own, ("row", "col"), axis=0, tiled=True),
        lax.all_gather(out_grad, ("row", "col"), axis=0, tiled=True),
    )
    projected = jnp.dot(normed_all, in_local, preferred_element_type=jnp.float32)
    paired = projected.reshape(group_tok, heads_dev, 2, head_width)
    gate_part = paired[:, :, 0, :].reshape(group_tok, inner_dev)
    inputs = paired[:, :, 1, :].reshape(group_tok, inner_dev)
    conv_inner = lax.dynamic_slice_in_dim(conv_taps, place * inner_dev, inner_dev, 1)
    conv_state = conv_taps[:, inner:]
    coefs = lax.dynamic_slice_in_dim(head_coef, place * heads_dev, heads_dev, 1)
    step_local = lax.dynamic_slice_in_dim(step_all, place * heads_dev, heads_dev, 1).astype(
        jnp.float32
    )
    gated, mixer_pull = jax.vjp(
        mixer_all,
        gate_part,
        inputs,
        state_all.astype(jnp.float32),
        step_local,
        conv_inner,
        conv_state,
        coefs,
    )
    squares = lax.psum(jnp.sum(gated * gated, axis=1), ("row", "col"))
    gated_rms = lax.rsqrt(squares / inner + NORM_EPS)[:, None]
    gain_local = lax.dynamic_slice_in_dim(gated_gain, place * inner_dev, inner_dev, 0)
    normed_out = (gated * gated_rms * gain_local[None, :]).astype(jnp.bfloat16)
    rows = normed_out
    mixed = lax.psum_scatter(
        jnp.dot(rows, out_local, preferred_element_type=jnp.float32),
        ("row", "col"),
        scatter_dimension=0,
        tiled=True,
    )
    block_out = (x_float + mixed).astype(jnp.bfloat16)
    grad_out_local = jnp.einsum(
        "tc,td->cd", normed_out, cotangent, preferred_element_type=jnp.float32
    )
    d_normed = jnp.einsum("td,cd->tc", cotangent, out_local, preferred_element_type=jnp.float32)
    gain_part = jnp.sum(d_normed * gated * gated_rms, axis=0)
    scaled = d_normed * gain_local[None, :]
    cross = lax.psum(jnp.sum(scaled * gated, axis=1), ("row", "col"))
    d_gated = gated_rms * scaled - gated * gated_rms**3 * (cross / inner)[:, None]
    d_gate, d_inputs, d_state, d_step, d_conv_inner, d_conv_state, d_coefs = mixer_pull(d_gated)
    d_projected = (
        jnp.stack(
            [
                d_gate.reshape(group_tok, heads_dev, head_width),
                d_inputs.reshape(group_tok, heads_dev, head_width),
            ],
            axis=2,
        )
        .reshape(group_tok, 2 * inner_dev)
        .astype(jnp.bfloat16)
    )
    grad_in_local = jnp.einsum(
        "td,tc->dc", normed_all, d_projected, preferred_element_type=jnp.float32
    )
    rows = d_projected
    d_normed_in = lax.psum_scatter(
        jnp.einsum("tc,dc->td", rows, in_local, preferred_element_type=jnp.float32),
        ("row", "col"),
        scatter_dimension=0,
        tiled=True,
    )
    step_spread = lax.dynamic_update_slice_in_dim(
        jnp.zeros((group_tok, head_total), jnp.float32), d_step, place * heads_dev, 1
    )
    state_back, step_back = (
        lax.psum_scatter(d_state, ("row", "col"), scatter_dimension=0, tiled=True),
        lax.psum_scatter(step_spread, ("row", "col"), scatter_dimension=0, tiled=True),
    )
    state_back = state_back.astype(jnp.bfloat16)
    step_back = step_back.astype(jnp.bfloat16)
    d_normed_in = (
        d_normed_in
        + jnp.einsum("tc,dc->td", state_back, state_full, preferred_element_type=jnp.float32)
        + jnp.einsum("tc,dc->td", step_back, step_full, preferred_element_type=jnp.float32)
    )
    grad_state_part = jnp.einsum(
        "td,tc->dc", normed_in, state_back, preferred_element_type=jnp.float32
    )
    grad_step_part = jnp.einsum(
        "td,tc->dc", normed_in, step_back, preferred_element_type=jnp.float32
    )
    grad_state, grad_step = (
        lax.psum_scatter(grad_state_part, ("dp", "row", "col"), scatter_dimension=0, tiled=True),
        lax.psum_scatter(grad_step_part, ("dp", "row", "col"), scatter_dimension=0, tiled=True),
    )
    grad_input, grad_output = (
        lax.psum_scatter(grad_in_local, "dp", scatter_dimension=0, tiled=True),
        lax.psum_scatter(grad_out_local, "dp", scatter_dimension=1, tiled=True),
    )
    scaled_in = d_normed_in * norm_gain[None, :]
    norm_part = jnp.sum(d_normed_in * x_float * inv_rms, axis=0)
    input_grad = (
        out_grad.astype(jnp.float32)
        + inv_rms * scaled_in
        - x_float * inv_rms**3 * jnp.mean(scaled_in * x_float, axis=1, keepdims=True)
    )
    gated_spread = lax.dynamic_update_slice_in_dim(
        jnp.zeros((inner,), jnp.float32), gain_part, place * inner_dev, 0
    )
    conv_front = lax.dynamic_update_slice_in_dim(
        jnp.zeros((5, inner), jnp.float32), d_conv_inner, place * inner_dev, 1
    )
    conv_spread = jnp.concatenate([conv_front, d_conv_state], axis=1)
    coef_spread = lax.dynamic_update_slice_in_dim(
        jnp.zeros((3, head_total), jnp.float32), d_coefs, place * heads_dev, 1
    )
    grad_norm, grad_gated, grad_conv, grad_coef = lax.psum(
        (norm_part, gated_spread, conv_spread, coef_spread), ("dp", "row", "col")
    )
    n_norm, f_norm, s_norm = adamw(
        norm_gain, grad_norm, first_norm_gain, second_norm_gain, VECTOR_RATE, 0.0
    )
    n_input, f_input, s_input = adamw(
        input_proj, grad_input, first_input_proj, second_input_proj, MATRIX_RATE, WEIGHT_DECAY
    )
    n_state, f_state, s_state = adamw(
        state_proj, grad_state, first_state_proj, second_state_proj, MATRIX_RATE, WEIGHT_DECAY
    )
    n_step, f_step, s_step = adamw(
        step_proj, grad_step, first_step_proj, second_step_proj, MATRIX_RATE, WEIGHT_DECAY
    )
    n_conv, f_conv, s_conv = adamw(
        conv_taps, grad_conv, first_conv_taps, second_conv_taps, VECTOR_RATE, 0.0
    )
    n_head, f_head, s_head = adamw(
        head_coef, grad_coef, first_head_coef, second_head_coef, VECTOR_RATE, 0.0
    )
    n_gated, f_gated, s_gated = adamw(
        gated_gain, grad_gated, first_gated_gain, second_gated_gain, VECTOR_RATE, 0.0
    )
    n_output, f_output, s_output = adamw(
        output_proj, grad_output, first_output_proj, second_output_proj, MATRIX_RATE, WEIGHT_DECAY
    )
    return (
        block_out,
        input_grad,
        grad_norm,
        grad_input,
        grad_state,
        grad_step,
        grad_conv,
        grad_coef,
        grad_gated,
        grad_output,
        n_norm,
        f_norm,
        s_norm,
        n_input,
        f_input,
        s_input,
        n_state,
        f_state,
        s_state,
        n_step,
        f_step,
        s_step,
        n_conv,
        f_conv,
        s_conv,
        n_head,
        f_head,
        s_head,
        n_gated,
        f_gated,
        s_gated,
        n_output,
        f_output,
        s_output,
    )


def solution(mesh):
    return jax.shard_map(
        per_device,
        mesh=mesh,
        in_specs=(
            P(("dp", "row", "col"), None),
            P(("dp", "row", "col"), None),
            P(),
            P(),
            P(),
            P("dp", ("row", "col")),
            P("dp", ("row", "col")),
            P("dp", ("row", "col")),
            P(("dp", "row", "col"), None),
            P(("dp", "row", "col"), None),
            P(("dp", "row", "col"), None),
            P(("dp", "row", "col"), None),
            P(("dp", "row", "col"), None),
            P(("dp", "row", "col"), None),
            P(),
            P(),
            P(),
            P(),
            P(),
            P(),
            P(),
            P(),
            P(),
            P(("row", "col"), "dp"),
            P(("row", "col"), "dp"),
            P(("row", "col"), "dp"),
        ),
        out_specs=(
            P(("dp", "row", "col"), None),
            P(("dp", "row", "col"), None),
            P(),
            P("dp", ("row", "col")),
            P(("dp", "row", "col"), None),
            P(("dp", "row", "col"), None),
            P(),
            P(),
            P(),
            P(("row", "col"), "dp"),
            P(),
            P(),
            P(),
            P("dp", ("row", "col")),
            P("dp", ("row", "col")),
            P("dp", ("row", "col")),
            P(("dp", "row", "col"), None),
            P(("dp", "row", "col"), None),
            P(("dp", "row", "col"), None),
            P(("dp", "row", "col"), None),
            P(("dp", "row", "col"), None),
            P(("dp", "row", "col"), None),
            P(),
            P(),
            P(),
            P(),
            P(),
            P(),
            P(),
            P(),
            P(),
            P(("row", "col"), "dp"),
            P(("row", "col"), "dp"),
            P(("row", "col"), "dp"),
        ),
        check_vma=False,
    )
```

profile of v0, /device:TPU:0, one launch (start us, length us, event | category | flops | bytes accessed | tf_op | source)
XLA Modules:
  0.0 1698.1 jit_solution(3342387534222917837)
XLA Ops:
  10.1 77.2 %all_gather.26 = bf16[1536,256]{1,0:T(8,128)(2,1)S(1)} all-gather(bf16[48,256]{1,0:T(8,128)(2,1)S(1)} %convert_element_type.58), channel_id=1, replica_groups=mesh['dp'=4,'row'=2,'col'=4] {'dp','row','col'}, dimensions={0}, use_global_device_ids=true | all-gather | bytes 811008 | tf_op jit(solution)/shard_map/all_gather | solution.py:147
  95.0 68.2 %all_gather.28 = bf16[1536,48]{1,0:T(8,128)(2,1)S(1)} all-gather(bf16[48,48]{1,0:T(8,128)(2,1)S(1)} %convert_element_type.60), channel_id=1, replica_groups=mesh['dp'=4,'row'=2,'col'=4] {'dp','row','col'}, dimensions={0}, use_global_device_ids=true | all-gather | bytes 152064 | tf_op jit(solution)/shard_map/all_gather | solution.py:148
  164.0 32.7 %all_gather.29 = bf16[2048,48]{0,1:T(8,128)(2,1)S(1)} all-gather(bf16[256,48]{0,1:T(8,128)(2,1)S(1)} %convolution_convert_fusion.1), channel_id=1, replica_groups=mesh['dp'=4,'row'=2,'col'=4] {'row','col'}, dimensions={0}, use_global_device_ids=true | all-gather | bytes 221184 | tf_op jit(solution)/shard_map/all_gather | solution.py:162
  202.5 55.3 %all-gather.6.cloned.1.call-done = bf16[2048,1536]{1,0:T(8,128)(2,1)} async-done(((bf16[256,1536]{1,0:T(8,128)(2,1)}), bf16[2048,1536]{1,0:T(8,128)(2,1)}) %all-gather.6.cloned.1.call-update) | async-done | bytes 6291472 | tf_op jit(solution)/shard_map/all_gather | solution.py:160
  283.0 75.7 %while.43 = (s32[]{:T(128)}, f32[2,1024,384]{1,2,0:T(8,128)}, f32[1,384]{1,0:T(1,128)S(1)}, f32[2,1024,384]{1,2,0:T(8,128)}, f32[1,384]{1,0:T(1,128)S(1)}, /*ind...) while((s32[]{:T(128)}, f32[2,1024,384]{1,2,0:T(8,128)}, ...), condition=%wide.region_4.5_spmd.clone.clone, body=%wide.region_1.4_spmd.clone.sunk.clone | while | flops 2843105280 | bytes 111481648 | solution.py:84
  362.7 19.9 %psum.42 = f32[2048]{0:T(1024)S(1)} all-reduce(f32[2048]{0:T(1024)S(1)} %bitcast.754), channel_id=1, replica_groups=mesh['dp'=4,'row'=2,'col'=4] {'row','col'}, use_global_device_ids=true, to_apply=%region_6.7 | all-reduce | flops 2048 | bytes 16384 | tf_op jit(solution)/shard_map/psum | solution.py:185
  382.7 10.2 fusion.138
  392.9 18.0 %psum.43 = f32[2048]{0:T(1024)S(1)} all-reduce(f32[2048]{0:T(1024)S(1)} %get-tuple-element.979), channel_id=1, replica_groups=mesh['dp'=4,'row'=2,'col'=4] {'row','col'}, use_global_device_ids=true, to_apply=%region_9.10 | all-reduce | flops 2048 | bytes 16384 | tf_op jit(solution)/shard_map/psum | solution.py:203
  417.3 292.8 %while.44 = (s32[]{:T(128)}, f32[5,384]{1,0:T(8,128)}, f32[5,256]{1,0:T(8,128)}, f32[3,6]{1,0:T(4,128)}, bf16[2,1024,384]{1,2,0:T(8,128)(2,1)}, /*index=5*/bf16[...) while((s32[]{:T(128)}, f32[5,384]{1,0:T(8,128)}, ...), condition=%wide.region_38.39_spmd.clone.clone, body=%wide.region_10.38_spmd.clone.sunk.clone | while | flops 8532760576 | bytes 316975616 | solution.py:84
  496.9 9.6 fusion.380
  511.5 30.6 %reduce-window.88 = f32[4,6,2,128]{3,2,1,0:T(2,128)S(1)} reduce-window(f32[4,6,2,128]{3,2,1,0:T(2,128)S(1)} %reshape.763, f32[]{:T(128)} %constant.263.clone.1..sunk.3), window={size=1x1x1x128 pad=0_0x0_0x0_0x0_127}, to_apply=%region_33.33 | reduce-window | flops 780288 | bytes 49156 | tf_op jit(solution)/shard_map/reduce-window.36
  639.5 9.6 fusion.380
  654.1 30.3 %reduce-window.88 = f32[4,6,2,128]{3,2,1,0:T(2,128)S(1)} reduce-window(f32[4,6,2,128]{3,2,1,0:T(2,128)S(1)} %reshape.763, f32[]{:T(128)} %constant.263.clone.1..sunk.3), window={size=1x1x1x128 pad=0_0x0_0x0_0x0_127}, to_apply=%region_33.33 | reduce-window | flops 780288 | bytes 49156 | tf_op jit(solution)/shard_map/reduce-window.36
  713.8 61.1 %reduce-scatter.15.cloned.1.call-done = f32[256,48]{0,1:T(8,128)} async-done(((f32[2048,48]{0,1:T(8,128)}), f32[256,48]{0,1:T(8,128)}) %reduce-scatter.15.cloned.1.call-update) | async-done | bytes 49168 | tf_op jit(solution)/shard_map/reduce_scatter | solution.py:232
  784.0 62.0 %reduce-scatter.13.cloned.1.call-done = f32[256,256]{1,0:T(8,128)} async-done(((f32[2048,256]{1,0:T(8,128)}), f32[256,256]{1,0:T(8,128)}) %reduce-scatter.13.cloned.1.call-update) | async-done | bytes 262160 | tf_op jit(solution)/shard_map/reduce_scatter | solution.py:231
  877.8 10.4 fusion.184
  896.9 76.9 %all-reduce.38.cloned.1.call-done = f32[5,3328]{1,0:T(8,128)} async-done(((f32[5,3328]{1,0:T(8,128)}), f32[5,3328]{1,0:T(8,128)}) %all-reduce.38.cloned.1.call-update) | async-done | bytes 66576 | tf_op jit(solution)/shard_map/psum | solution.py:272
  975.5 101.2 %reduce-scatter.21.cloned.1.call-done = f32[48,48]{1,0:T(8,128)} async-done(((f32[1536,48]{1,0:T(8,128)}), f32[48,48]{1,0:T(8,128)}) %reduce-scatter.21.cloned.1.call-update) | async-done | bytes 9232 | tf_op jit(solution)/shard_map/reduce_scatter | solution.py:249
  1078.0 33.4 %reduce-scatter.23.cloned.1.call-done = f32[384,384]{1,0:T(8,128)} async-done(((f32[384,1536]{1,0:T(8,128)}), f32[384,384]{1,0:T(8,128)}) %reduce-scatter.23.cloned.1.call-update) | async-done | bytes 589840 | tf_op jit(solution)/shard_map/reduce_scatter | solution.py:253
  1114.0 101.3 %reduce-scatter.19.cloned.1.call-done = f32[48,256]{1,0:T(8,128)} async-done(((f32[1536,256]{1,0:T(8,128)}), f32[48,256]{1,0:T(8,128)}) %reduce-scatter.19.cloned.1.call-update) | async-done | bytes 49168 | tf_op jit(solution)/shard_map/reduce_scatter | solution.py:248
  1216.7 48.5 %reduce-scatter.17.cloned.1.call-done = f32[384,768]{1,0:T(8,128)} async-done(((f32[1536,768]{1,0:T(8,128)}), f32[384,768]{1,0:T(8,128)}) %reduce-scatter.17.cloned.1.call-update) | async-done | bytes 1179664 | tf_op jit(solution)/shard_map/reduce_scatter | solution.py:252
  1269.6 206.7 %reduce-scatter.11.cloned.1.call-done = f32[256,1536]{1,0:T(8,128)} async-done(((f32[2048,1536]{1,0:T(8,128)}), f32[256,1536]{1,0:T(8,128)}) %reduce-scatter.11.cloned.1.call-update) | async-done | bytes 1572880 | tf_op jit(solution)/shard_map/reduce_scatter | solution.py:221
  1479.5 43.5 %all-reduce.35 = (f32[1536]{0:T(1024)S(1)}, f32[3,48]{1,0:T(4,128)S(1)}, f32[3072]{0:T(1024)S(1)}) all-reduce(f32[1536]{0:T(1024)S(1)} %get-tuple-element.980, f32[3,48]{1,0:T(4,128)} %copy-done.151, f32[3072]{0:T(1024)} %copy-done.141), channel_id=1, replica_groups=mesh['dp'=4,'row'=2,'col'=4] {'dp','row','col'}, use_global_device_ids=true, to_apply=%region_44.45 | all-reduce | flops 4752 | bytes 38016 | tf_op jit(solution)/shard_map/psum | solution.py:272
  1527.7 159.6 %reduce-scatter.9.cloned.1.call-done = f32[256,1536]{1,0:T(8,128)} async-done(((f32[2048,1536]{1,0:T(8,128)}), f32[256,1536]{1,0:T(8,128)}) %reduce-scatter.9.cloned.1.call-update) | async-done | bytes 1572880 | tf_op jit(solution)/shard_map/reduce_scatter | solution.py:190
  (893 shorter events, 405.2 us)
Async XLA Ops:
  7.2 192.5 %all-gather.10.cloned.1.call-start = ((), (), s32[]{:S(2)}) async-start(), calls=%async_computation.10 | async-start | bytes 1179648 | tf_op jit(solution)/shard_map/all_gather | solution.py:161
  88.7 113.8 %all-gather.8.cloned.1.call-start = ((), (), s32[]{:S(2)}) async-start(), calls=%async_computation.9 | async-start | bytes 2949120 | tf_op jit(solution)/shard_map/all_gather | solution.py:143
  90.1 167.6 %all-gather.6.cloned.1.call-start = ((), (), s32[]{:S(2)}) async-start(), calls=%async_computation.8 | async-start | bytes 7077888 | tf_op jit(solution)/shard_map/all_gather | solution.py:160
  90.8 291.8 %all-gather.12.cloned.1.call-start = ((), (), s32[]{:S(2)}) async-start(), calls=%async_computation.11 | async-start | bytes 1474560 | tf_op jit(solution)/shard_map/all_gather | solution.py:144
  91.7 291.0 %all-gather.14.cloned.1.call-start = ((), (), s32[]{:S(2)}) async-start(), calls=%async_computation.13 | async-start | bytes 7077888 | tf_op jit(solution)/shard_map/all_gather | solution.py:163
  92.3 682.6 %reduce-scatter.15.cloned.1.call-start = ((), (), s32[]{:S(2)}) async-start(), calls=%async_computation.16 | async-start | bytes 442368 | tf_op jit(solution)/shard_map/reduce_scatter | solution.py:232
  712.2 133.8 %reduce-scatter.13.cloned.1.call-start = ((), (), s32[]{:S(2)}) async-start(), calls=%async_computation.15 | async-start | bytes 2359296 | tf_op jit(solution)/shard_map/reduce_scatter | solution.py:231
  713.0 260.8 %all-reduce.38.cloned.1.call-start = ((), (), s32[]{:S(2)}) async-start(), calls=%async_computation.20 | async-start | bytes 212992 | tf_op jit(solution)/shard_map/psum | solution.py:272
  713.8 362.9 %reduce-scatter.21.cloned.1.call-start = ((), (), s32[]{:S(2)}) async-start(), calls=%async_computation.19 | async-start | bytes 811008 | tf_op jit(solution)/shard_map/reduce_scatter | solution.py:249
  777.0 334.4 %reduce-scatter.23.cloned.1.call-start = ((), (), s32[]{:S(2)}) async-start(), calls=%async_computation.21 | async-start | bytes 2949120 | tf_op jit(solution)/shard_map/reduce_scatter | solution.py:253
  783.9 431.3 %reduce-scatter.19.cloned.1.call-start = ((), (), s32[]{:S(2)}) async-start(), calls=%async_computation.18 | async-start | bytes 1622016 | tf_op jit(solution)/shard_map/reduce_scatter | solution.py:248
  848.5 416.7 %reduce-scatter.17.cloned.1.call-start = ((), (), s32[]{:S(2)}) async-start(), calls=%async_computation.17 | async-start | bytes 5898240 | tf_op jit(solution)/shard_map/reduce_scatter | solution.py:252
  877.8 598.6 %reduce-scatter.11.cloned.1.call-start = ((), (), s32[]{:S(2)}) async-start(), calls=%async_computation.14 | async-start | bytes 14155776 | tf_op jit(solution)/shard_map/reduce_scatter | solution.py:221
  888.2 799.1 %reduce-scatter.9.cloned.1.call-start = ((), (), s32[]{:S(2)}) async-start(), calls=%async_computation.12 | async-start | bytes 14155776 | tf_op jit(solution)/shard_map/reduce_scatter | solution.py:190
  895.9 215.6 %copy-start.77 = (f32[384,384]{1,0:T(8,128)S(1)}, f32[384,384]{1,0:T(8,128)}, u32[]{:S(2)}) copy-start(f32[384,384]{1,0:T(8,128)} %param.53) | copy-start | bytes 1769476
  895.9 215.6 %copy-start.87 = (f32[384,384]{1,0:T(8,128)S(1)}, f32[384,384]{1,0:T(8,128)}, u32[]{:S(2)}) copy-start(f32[384,384]{1,0:T(8,128)} %param.54) | copy-start | bytes 1769476
  895.9 215.6 %copy-start.88 = (f32[384,384]{1,0:T(8,128)S(1)}, f32[384,384]{1,0:T(8,128)}, u32[]{:S(2)}) copy-start(f32[384,384]{1,0:T(8,128)} %param.55) | copy-start | bytes 1769476
  896.7 217.3 %copy-start.141 = (f32[3072]{0:T(1024)}, f32[3072]{0:T(1024)S(1)}, u32[]{:S(2)}) copy-start(f32[3072]{0:T(1024)S(1)} %dynamic_update_slice.62) | copy-start | bytes 36868
  1216.7 259.6 %copy-start.63 = (bf16[1536,256]{1,0:T(8,128)(2,1)S(1)}, bf16[1536,256]{1,0:T(8,128)(2,1)}, u32[]{:S(2)}) copy-start(bf16[1536,256]{1,0:T(8,128)(2,1)} %copy-done.62) | copy-start | bytes 2359300
  1216.7 259.6 %copy-start.84 = (f32[256,256]{1,0:T(8,128)S(1)}, f32[256,256]{1,0:T(8,128)}, u32[]{:S(2)}) copy-start(f32[256,256]{1,0:T(8,128)} %reduce-scatter.13.cloned.1.call-done) | copy-start | bytes 786436
  1269.6 208.6 %copy-start.52 = (bf16[256,1536]{1,0:T(8,128)(2,1)S(1)}, bf16[256,1536]{1,0:T(8,128)(2,1)}, u32[]{:S(2)}) copy-start(bf16[256,1536]{1,0:T(8,128)(2,1)} %param.30) | copy-start | bytes 2359300
  1269.6 208.6 %copy-start.69 = (bf16[1536,48]{1,0:T(8,128)(2,1)S(1)}, bf16[1536,48]{1,0:T(8,128)(2,1)}, u32[]{:S(2)}) copy-start(bf16[1536,48]{1,0:T(8,128)(2,1)} %copy-done.68) | copy-start | bytes 442372
  1269.6 208.6 %copy-start.124 = (f32[1536]{0:T(1024)S(1)}, f32[1536]{0:T(1024)}, u32[]{:S(2)}) copy-start(f32[1536]{0:T(1024)} %param.32) | copy-start | bytes 18436
  1478.2 209.1 %copy-start.72 = (bf16[256,1536]{1,0:T(8,128)(2,1)S(1)}, bf16[256,1536]{1,0:T(8,128)(2,1)}, u32[]{:S(2)}) copy-start(bf16[256,1536]{1,0:T(8,128)(2,1)} %param.31) | copy-start | bytes 2359300
  (248 other events, 3499.7 us)
Sparse Core Ops, SparseCore 0:
  88.8 38.3 all-gather.9
  129.3 23.3 all-gather.7
  155.3 102.3 all-gather.5
  259.7 15.6 all-gather.11
  277.3 99.5 all-gather.13
  712.3 62.5 reduce-scatter.14
  778.4 67.5 reduce-scatter.12
  852.1 121.6 all-reduce.37
  979.5 97.1 reduce-scatter.20
  1079.6 31.8 reduce-scatter.22
  1117.3 97.9 reduce-scatter.18
  1218.2 47.0 reduce-scatter.16
  1268.9 207.4 reduce-scatter.10
  1479.8 207.4 reduce-scatter.8
where the time goes:
time: 1710 us; the launch traced here: 1700 us
  waiting for transfers between devices  908 us (53%)
  blocking collectives  260 us (15%)
  other arithmetic  195 us (11%)
  matrix products  170 us (10%)
  local copies, waits for them, and re-layouts  138 us (8%)
    reduce_scatter x1, waiting for transfers between devices, per_device(): lax.psum_scatter(jnp.einsum('tc,dc->td', rows, in_local, preferred_elemen...  207 us
    reduce_scatter x1, waiting for transfers between devices, per_device(): lax.psum_scatter(jnp.dot(rows, out_local, preferred_element_type=jnp.floa...  160 us
    reduce_scatter x1, waiting for transfers between devices, per_device(): lax.psum_scatter(grad_state_part, ('dp', 'row', 'col'), scatter_dimension...  101 us
    reduce_scatter x1, waiting for transfers between devices, per_device(): lax.psum_scatter(grad_step_part, ('dp', 'row', 'col'), scatter_dimension=...  101 us
    another operation x25, other arithmetic  91 us
    all_gather x1, blocking collectives, per_device(): lax.all_gather(state_proj.astype(jnp.bfloat16), ('dp', 'row', 'col'), axi...  77.2 us
    psum x1, waiting for transfers between devices, per_device(): lax.psum((norm_part, gated_spread, conv_spread, coef_spread), ('dp', 'row...  76.9 us
    all_gather x1, blocking collectives, per_device(): lax.all_gather(step_proj.astype(jnp.bfloat16), ('dp', 'row', 'col'), axis...  68.2 us
  transfers between devices with their start and end apart: 14, of which 10 were waited for; matrix products, arithmetic and copies ran while one was open for 10% of the time, Pallas kernels for 0%

commit v1 on v0

--- a/solution.py
+++ b/solution.py
@@ -14,6 +14,18 @@
 MATRIX_RATE = 0.003
 VECTOR_RATE = 0.1
 WEIGHT_DECAY = 0.1
+
+
+def collect(value, axis, dim):
+    ways, here, step = (lax.axis_size(axis), lax.axis_index(axis), value.shape[dim])
+    line, have = (value, 1)
+    while have < ways:
+        line = jnp.concatenate(
+            [line, lax.ppermute(line, axis, [(d, (d - have) % ways) for d in range(ways)])],
+            axis=dim,
+        )
+        have = 2 * have
+    return jnp.roll(line, here * step, axis=dim)
 
 
 def causal_conv(values, filters):
@@ -157,7 +169,7 @@
         jnp.bfloat16
     )
     normed_all, state_all, step_all, cotangent = (
-        lax.all_gather(normed_in, ("row", "col"), axis=0, tiled=True),
+        collect(normed_in, ("row", "col"), 0),
         lax.all_gather(state_own, ("row", "col"), axis=0, tiled=True),
         lax.all_gather(step_own, ("row", "col"), axis=0, tiled=True),
         lax.all_gather(out_grad, ("row", "col"), axis=0, tiled=True),

time: 1710 us -> 1770 us (1.035)
  waiting for transfers between devices: 908 us -> 939 us
    ppermute x0 -> x3, waiting for transfers between devices: none -> 87.1 us  [collect(): lax.ppermute(line, axis, [(d, (d - have) % ways) for d in range(ways)])]
    all_gather x1 -> x0, waiting for transfers between devices: 55.3 us -> none  [per_device(): lax.all_gather(normed_in, ('row', 'col'), axis=0, tiled=True)]
  transfers between devices with their start and end apart: 14 -> 16, of which waited for: 10 -> 11; matrix products, arithmetic and copies ran while one was open for 10% -> 11% of each run, Pallas kernels for 0% -> 0%
where the time goes in v1:
time: 1770 us; the launch traced here: 1760 us
  waiting for transfers between devices  939 us (53%)
  blocking collectives  265 us (15%)
  other arithmetic  199 us (11%)
  matrix products  170 us (10%)
  local copies, waits for them, and re-layouts  151 us (9%)
    reduce_scatter x1, waiting for transfers between devices, per_device(): lax.psum_scatter(jnp.einsum('tc,dc->td', rows, in_local, preferred_elemen...  207 us
    reduce_scatter x1, waiting for transfers between devices, per_device(): lax.psum_scatter(jnp.dot(rows, out_local, preferred_element_type=jnp.floa...  160 us
    reduce_scatter x1, waiting for transfers between devices, per_device(): lax.psum_scatter(grad_step_part, ('dp', 'row', 'col'), scatter_dimension=...  102 us
    reduce_scatter x1, waiting for transfers between devices, per_device(): lax.psum_scatter(grad_state_part, ('dp', 'row', 'col'), scatter_dimension...  101 us
    another operation x25, other arithmetic  91 us
    ppermute x3, waiting for transfers between devices, collect(): lax.ppermute(line, axis, [(d, (d - have) % ways) for d in range(ways)])  87.1 us
    all_gather x1, blocking collectives, per_device(): lax.all_gather(state_proj.astype(jnp.bfloat16), ('dp', 'row', 'col'), axi...  77.3 us
    psum x1, waiting for transfers between devices, per_device(): lax.psum((norm_part, gated_spread, conv_spread, coef_spread), ('dp', 'row...  77.2 us
  transfers between devices with their start and end apart: 16, of which 11 were waited for; matrix products, arithmetic and copies ran while one was open for 11% of the time, Pallas kernels for 0%

profile of v1, /device:TPU:0, one launch (start us, length us, event | category | flops | bytes accessed | tf_op | source)
XLA Modules:
  0.0 1762.9 jit_solution(6667814103692262516)
XLA Ops:
  10.1 77.3 %all_gather.22 = bf16[1536,256]{1,0:T(8,128)(2,1)S(1)} all-gather(bf16[48,256]{1,0:T(8,128)(2,1)S(1)} %convert_element_type.58), channel_id=1, replica_groups=mesh['dp'=4,'row'=2,'col'=4] {'dp','row','col'}, dimensions={0}, use_global_device_ids=true | all-gather | bytes 811008 | tf_op jit(solution)/shard_map/all_gather | solution.py:159
  90.7 20.7 %collective-permute-done = bf16[256,1536]{1,0:T(8,128)(2,1)S(1)} collective-permute-done((bf16[256,1536]{1,0:T(8,128)(2,1)S(1)}, bf16[256,1536]{1,0:T(8,128)(2,1)S(1)}, u32[]{:S(2)}, u32[]{:S(2)}) %collective-permute-start) | collective-permute-done | bytes 786464 | tf_op jit(solution)/shard_map/ppermute | solution.py:24
  114.6 66.5 %collective-permute-done.1 = bf16[512,1536]{1,0:T(8,128)(2,1)S(1)} collective-permute-done((bf16[512,1536]{1,0:T(8,128)(2,1)}, bf16[512,1536]{1,0:T(8,128)(2,1)S(1)}, u32[]{:S(2)}, u32[]{:S(2)}) %collective-permute-start.1) | collective-permute-done | bytes 1572896 | tf_op jit(solution)/shard_map/ppermute | solution.py:24
  182.9 10.3 collective-permute-start.2
  196.5 73.6 %all_gather.24 = bf16[1536,48]{1,0:T(8,128)(2,1)S(1)} all-gather(bf16[48,48]{1,0:T(8,128)(2,1)S(1)} %convert_element_type.60), channel_id=1, replica_groups=mesh['dp'=4,'row'=2,'col'=4] {'dp','row','col'}, dimensions={0}, use_global_device_ids=true | all-gather | bytes 152064 | tf_op jit(solution)/shard_map/all_gather | solution.py:160
  271.2 32.7 %all_gather.25 = bf16[2048,48]{0,1:T(8,128)(2,1)S(1)} all-gather(bf16[256,48]{0,1:T(8,128)(2,1)S(1)} %convolution_convert_fusion.1), channel_id=1, replica_groups=mesh['dp'=4,'row'=2,'col'=4] {'row','col'}, dimensions={0}, use_global_device_ids=true | all-gather | bytes 221184 | tf_op jit(solution)/shard_map/all_gather | solution.py:174
  348.5 75.6 %while.43 = (s32[]{:T(128)}, f32[2,1024,384]{1,2,0:T(8,128)}, f32[1,384]{1,0:T(1,128)S(1)}, f32[2,1024,384]{1,2,0:T(8,128)}, f32[1,384]{1,0:T(1,128)S(1)}, /*ind...) while((s32[]{:T(128)}, f32[2,1024,384]{1,2,0:T(8,128)}, ...), condition=%wide.region_4.5_spmd.clone.clone, body=%wide.region_1.4_spmd.clone.sunk.clone | while | flops 2843105280 | bytes 111481648 | solution.py:96
  428.1 17.7 %psum.42 = f32[2048]{0:T(1024)S(1)} all-reduce(f32[2048]{0:T(1024)S(1)} %bitcast.752), channel_id=1, replica_groups=mesh['dp'=4,'row'=2,'col'=4] {'row','col'}, use_global_device_ids=true, to_apply=%region_6.7 | all-reduce | flops 2048 | bytes 16384 | tf_op jit(solution)/shard_map/psum | solution.py:197
  445.9 10.1 fusion.142
  456.0 20.2 %psum.43 = f32[2048]{0:T(1024)S(1)} all-reduce(f32[2048]{0:T(1024)S(1)} %get-tuple-element.979), channel_id=1, replica_groups=mesh['dp'=4,'row'=2,'col'=4] {'row','col'}, use_global_device_ids=true, to_apply=%region_9.10 | all-reduce | flops 2048 | bytes 16384 | tf_op jit(solution)/shard_map/psum | solution.py:215
  482.4 292.7 %while.44 = (s32[]{:T(128)}, f32[5,384]{1,0:T(8,128)}, f32[5,256]{1,0:T(8,128)}, f32[3,6]{1,0:T(4,128)}, bf16[2,1024,384]{1,2,0:T(8,128)(2,1)}, /*index=5*/bf16[...) while((s32[]{:T(128)}, f32[5,384]{1,0:T(8,128)}, ...), condition=%wide.region_38.39_spmd.clone.clone, body=%wide.region_10.38_spmd.clone.sunk.clone | while | flops 8532760576 | bytes 316975616 | solution.py:96
  576.5 30.6 %reduce-window.88 = f32[4,6,2,128]{3,2,1,0:T(2,128)S(1)} reduce-window(f32[4,6,2,128]{3,2,1,0:T(2,128)S(1)} %reshape.763, f32[]{:T(128)} %constant.282.clone.1..sunk.3), window={size=1x1x1x128 pad=0_0x0_0x0_0x0_127}, to_apply=%region_33.33 | reduce-window | flops 780288 | bytes 49156 | tf_op jit(solution)/shard_map/reduce-window.36
  719.1 30.3 %reduce-window.88 = f32[4,6,2,128]{3,2,1,0:T(2,128)S(1)} reduce-window(f32[4,6,2,128]{3,2,1,0:T(2,128)S(1)} %reshape.763, f32[]{:T(128)} %constant.282.clone.1..sunk.3), window={size=1x1x1x128 pad=0_0x0_0x0_0x0_127}, to_apply=%region_33.33 | reduce-window | flops 780288 | bytes 49156 | tf_op jit(solution)/shard_map/reduce-window.36
  778.6 60.5 %reduce-scatter.15.cloned.1.call-done = f32[256,48]{0,1:T(8,128)} async-done(((f32[2048,48]{0,1:T(8,128)}), f32[256,48]{0,1:T(8,128)}) %reduce-scatter.15.cloned.1.call-update) | async-done | bytes 49168 | tf_op jit(solution)/shard_map/reduce_scatter | solution.py:244
  848.3 61.9 %reduce-scatter.13.cloned.1.call-done = f32[256,256]{1,0:T(8,128)} async-done(((f32[2048,256]{1,0:T(8,128)}), f32[256,256]{1,0:T(8,128)}) %reduce-scatter.13.cloned.1.call-update) | async-done | bytes 262160 | tf_op jit(solution)/shard_map/reduce_scatter | solution.py:243
  941.7 10.4 fusion.190
  960.7 77.2 %all-reduce.38.cloned.1.call-done = f32[5,3328]{1,0:T(8,128)} async-done(((f32[5,3328]{1,0:T(8,128)}), f32[5,3328]{1,0:T(8,128)}) %all-reduce.38.cloned.1.call-update) | async-done | bytes 66576 | tf_op jit(solution)/shard_map/psum | solution.py:284
  1039.6 101.7 %reduce-scatter.21.cloned.1.call-done = f32[48,48]{1,0:T(8,128)} async-done(((f32[1536,48]{1,0:T(8,128)}), f32[48,48]{1,0:T(8,128)}) %reduce-scatter.21.cloned.1.call-update) | async-done | bytes 9232 | tf_op jit(solution)/shard_map/reduce_scatter | solution.py:261
  1142.7 33.6 %reduce-scatter.23.cloned.1.call-done = f32[384,384]{1,0:T(8,128)} async-done(((f32[384,1536]{1,0:T(8,128)}), f32[384,384]{1,0:T(8,128)}) %reduce-scatter.23.cloned.1.call-update) | async-done | bytes 589840 | tf_op jit(solution)/shard_map/reduce_scatter | solution.py:265
  1178.8 101.1 %reduce-scatter.19.cloned.1.call-done = f32[48,256]{1,0:T(8,128)} async-done(((f32[1536,256]{1,0:T(8,128)}), f32[48,256]{1,0:T(8,128)}) %reduce-scatter.19.cloned.1.call-update) | async-done | bytes 49168 | tf_op jit(solution)/shard_map/reduce_scatter | solution.py:260
  1281.4 48.7 %reduce-scatter.17.cloned.1.call-done = f32[384,768]{1,0:T(8,128)} async-done(((f32[1536,768]{1,0:T(8,128)}), f32[384,768]{1,0:T(8,128)}) %reduce-scatter.17.cloned.1.call-update) | async-done | bytes 1179664 | tf_op jit(solution)/shard_map/reduce_scatter | solution.py:264
  1334.5 206.6 %reduce-scatter.11.cloned.1.call-done = f32[256,1536]{1,0:T(8,128)} async-done(((f32[2048,1536]{1,0:T(8,128)}), f32[256,1536]{1,0:T(8,128)}) %reduce-scatter.11.cloned.1.call-update) | async-done | bytes 1572880 | tf_op jit(solution)/shard_map/reduce_scatter | solution.py:233
  1544.2 43.4 %all-reduce.35 = (f32[1536]{0:T(1024)S(1)}, f32[3,48]{1,0:T(4,128)S(1)}, f32[3072]{0:T(1024)S(1)}) all-reduce(f32[1536]{0:T(1024)S(1)} %get-tuple-element.980, f32[3,48]{1,0:T(4,128)} %copy-done.150, f32[3072]{0:T(1024)} %copy-done.140), channel_id=1, replica_groups=mesh['dp'=4,'row'=2,'col'=4] {'dp','row','col'}, use_global_device_ids=true, to_apply=%region_44.45 | all-reduce | flops 4752 | bytes 38016 | tf_op jit(solution)/shard_map/psum | solution.py:284
  1592.4 159.7 %reduce-scatter.9.cloned.1.call-done = f32[256,1536]{1,0:T(8,128)} async-done(((f32[2048,1536]{1,0:T(8,128)}), f32[256,1536]{1,0:T(8,128)}) %reduce-scatter.9.cloned.1.call-update) | async-done | bytes 1572880 | tf_op jit(solution)/shard_map/reduce_scatter | solution.py:202
  (903 shorter events, 441.5 us)
Async XLA Ops:
  7.2 301.1 %all-gather.7.cloned.1.call-start = ((), (), s32[]{:S(2)}) async-start(), calls=%async_computation.9 | async-start | bytes 1179648 | tf_op jit(solution)/shard_map/all_gather | solution.py:173
  88.6 227.7 %copy-start.28 = (bf16[256,1536]{1,0:T(8,128)(2,1)}, bf16[256,1536]{1,0:T(8,128)(2,1)S(1)}, u32[]{:S(2)}) copy-start(bf16[256,1536]{1,0:T(8,128)(2,1)S(1)} %get-tuple-element.1099) | copy-start | bytes 2359300
  89.6 233.5 %all-gather.5.cloned.1.call-start = ((), (), s32[]{:S(2)}) async-start(), calls=%async_computation.8 | async-start | bytes 2949120 | tf_op jit(solution)/shard_map/all_gather | solution.py:155
  90.6 355.3 %all-gather.9.cloned.1.call-start = ((), (), s32[]{:S(2)}) async-start(), calls=%async_computation.10 | async-start | bytes 1474560 | tf_op jit(solution)/shard_map/all_gather | solution.py:156
  90.6 20.7 %collective-permute-start = (bf16[256,1536]{1,0:T(8,128)(2,1)S(1)}, bf16[256,1536]{1,0:T(8,128)(2,1)S(1)}, u32[]{:S(2)}, u32[]{:S(2)}) collective-permute-start(bf16[256,1536]{1,0:T(8,128)(2,1)S(1)} %get-tuple-element.1099), channel_id=1, source_target_pairs={{0,7},{1,0},{2,1},{3,2},{4,3},{5,4},{6,5},{7,6},{8,15},{9,8},{10,9... | collective-permute-start | bytes 2359304 | tf_op jit(solution)/shard_map/ppermute | solution.py:24
  112.6 68.4 %collective-permute-start.1 = (bf16[512,1536]{1,0:T(8,128)(2,1)}, bf16[512,1536]{1,0:T(8,128)(2,1)S(1)}, u32[]{:S(2)}, u32[]{:S(2)}) collective-permute-start(bf16[512,1536]{1,0:T(8,128)(2,1)} %pad_maximum_fusion.5), channel_id=1, source_target_pairs={{0,6},{1,7},{2,0},{3,1},{4,2},{5,3},{6,4},{7,5},{8,14},{9,15},{10,... | collective-permute-start | bytes 4718600 | tf_op jit(solution)/shard_map/ppermute | solution.py:24
  114.5 331.3 %all-gather.11.cloned.1.call-start = ((), (), s32[]{:S(2)}) async-start(), calls=%async_computation.12 | async-start | bytes 7077888 | tf_op jit(solution)/shard_map/all_gather | solution.py:175
  182.9 129.5 %collective-permute-start.2 = (bf16[1024,1536]{1,0:T(8,128)(2,1)}, bf16[1024,1536]{1,0:T(8,128)(2,1)}, u32[]{:S(2)}, u32[]{:S(2)}) collective-permute-start(bf16[1024,1536]{1,0:T(8,128)(2,1)} %pad_maximum_fusion.3), channel_id=1, source_target_pairs={{0,4},{1,5},{2,6},{3,7},{4,0},{5,1},{6,2},{7,3},{8,12},{9,13},{10,... | collective-permute-start | bytes 9437192 | tf_op jit(solution)/shard_map/ppermute | solution.py:24
  193.2 646.0 %reduce-scatter.15.cloned.1.call-start = ((), (), s32[]{:S(2)}) async-start(), calls=%async_computation.15 | async-start | bytes 442368 | tf_op jit(solution)/shard_map/reduce_scatter | solution.py:244
  777.2 133.0 %reduce-scatter.13.cloned.1.call-start = ((), (), s32[]{:S(2)}) async-start(), calls=%async_computation.14 | async-start | bytes 2359296 | tf_op jit(solution)/shard_map/reduce_scatter | solution.py:243
  777.8 260.1 %all-reduce.38.cloned.1.call-start = ((), (), s32[]{:S(2)}) async-start(), calls=%async_computation.19 | async-start | bytes 212992 | tf_op jit(solution)/shard_map/psum | solution.py:284
  778.6 362.7 %reduce-scatter.21.cloned.1.call-start = ((), (), s32[]{:S(2)}) async-start(), calls=%async_computation.18 | async-start | bytes 811008 | tf_op jit(solution)/shard_map/reduce_scatter | solution.py:261
  841.3 335.0 %reduce-scatter.23.cloned.1.call-start = ((), (), s32[]{:S(2)}) async-start(), calls=%async_computation.20 | async-start | bytes 2949120 | tf_op jit(solution)/shard_map/reduce_scatter | solution.py:265
  848.2 431.7 %reduce-scatter.19.cloned.1.call-start = ((), (), s32[]{:S(2)}) async-start(), calls=%async_computation.17 | async-start | bytes 1622016 | tf_op jit(solution)/shard_map/reduce_scatter | solution.py:260
  912.7 417.4 %reduce-scatter.17.cloned.1.call-start = ((), (), s32[]{:S(2)}) async-start(), calls=%async_computation.16 | async-start | bytes 5898240 | tf_op jit(solution)/shard_map/reduce_scatter | solution.py:264
  941.7 599.3 %reduce-scatter.11.cloned.1.call-start = ((), (), s32[]{:S(2)}) async-start(), calls=%async_computation.13 | async-start | bytes 14155776 | tf_op jit(solution)/shard_map/reduce_scatter | solution.py:233
  952.1 800.0 %reduce-scatter.9.cloned.1.call-start = ((), (), s32[]{:S(2)}) async-start(), calls=%async_computation.11 | async-start | bytes 14155776 | tf_op jit(solution)/shard_map/reduce_scatter | solution.py:202
  959.7 216.6 %copy-start.76 = (f32[384,384]{1,0:T(8,128)S(1)}, f32[384,384]{1,0:T(8,128)}, u32[]{:S(2)}) copy-start(f32[384,384]{1,0:T(8,128)} %param.53) | copy-start | bytes 1769476
  959.7 216.5 %copy-start.86 = (f32[384,384]{1,0:T(8,128)S(1)}, f32[384,384]{1,0:T(8,128)}, u32[]{:S(2)}) copy-start(f32[384,384]{1,0:T(8,128)} %param.54) | copy-start | bytes 1769476
  959.8 216.5 %copy-start.87 = (f32[384,384]{1,0:T(8,128)S(1)}, f32[384,384]{1,0:T(8,128)}, u32[]{:S(2)}) copy-start(f32[384,384]{1,0:T(8,128)} %param.55) | copy-start | bytes 1769476
  960.5 218.3 %copy-start.140 = (f32[3072]{0:T(1024)}, f32[3072]{0:T(1024)S(1)}, u32[]{:S(2)}) copy-start(f32[3072]{0:T(1024)S(1)} %dynamic_update_slice.62) | copy-start | bytes 36868
  1281.4 259.6 %copy-start.62 = (bf16[1536,256]{1,0:T(8,128)(2,1)S(1)}, bf16[1536,256]{1,0:T(8,128)(2,1)}, u32[]{:S(2)}) copy-start(bf16[1536,256]{1,0:T(8,128)(2,1)} %copy-done.61) | copy-start | bytes 2359300
  1281.4 259.6 %copy-start.83 = (f32[256,256]{1,0:T(8,128)S(1)}, f32[256,256]{1,0:T(8,128)}, u32[]{:S(2)}) copy-start(f32[256,256]{1,0:T(8,128)} %reduce-scatter.13.cloned.1.call-done) | copy-start | bytes 786436
  1542.9 209.2 %copy-start.71 = (bf16[256,1536]{1,0:T(8,128)(2,1)S(1)}, bf16[256,1536]{1,0:T(8,128)(2,1)}, u32[]{:S(2)}) copy-start(bf16[256,1536]{1,0:T(8,128)(2,1)} %param.31) | copy-start | bytes 2359300
  (249 other events, 4088.2 us)
Sparse Core Ops, SparseCore 0:
  89.7 74.9 all-gather.6
  166.9 41.2 all-gather.4
  210.3 17.8 all-gather.8
  230.1 104.0 all-gather.10
  777.3 61.7 reduce-scatter.14
  842.6 67.5 reduce-scatter.12
  916.3 121.5 all-reduce.37
  1044.1 97.1 reduce-scatter.20
  1144.4 31.8 reduce-scatter.22
  1181.9 97.9 reduce-scatter.18
  1283.1 47.0 reduce-scatter.16
  1333.6 207.4 reduce-scatter.10
  1544.6 207.4 reduce-scatter.8
